TPU v7x, 32 devices: a whole 2x2x4 slice. The times are simulated.
32 devices in a mesh: exp: 4 (over z), row: 4 (over y, core), col: 2 (over x).
Axes of the slice: x: 2, y: 2, z: 4, core: 2. Of those that a mesh axis runs over, the one named last changes fastest.
Arguments:
- exposures: float32 [64, 128, 1024], P('exp', 'row', 'col'), may hold values from -6 to 6
- bad_pixels: int32 [64, 128, 1024], P('exp', 'row', 'col'), may hold values 0 or 1
- offsets: int32 [64, 2], P('exp'), may hold values from -8 to 8, as said below
- warp_index: int32 [64, 2], P('exp'), may hold values from 0 to 15
- blur_index: int32 [64], P('exp'), may hold values from 0 to 7
Outputs:
- residual: float32 [64, 128, 1024], P('exp', 'row', 'col')
- median_sky: float32 [128, 1024], P('row', 'col')
Inputs may be any that keep to these rules, and one draw needn't show every extreme that they name: `offsets`: in each component some exposure has the offset -8 and some has 8.
All inputs are finite; a program needn't handle non-finite values. No bound on the sum of `bad_pixels` on one device may be relied on, other than what follows from the above.
Results may differ from a plain program's by a relative error of at most 0.0003.
Values sent between devices are 32-bit elements; how exact they have to be, the bound alone decides.
No kernel may reach another device: no remote copies, remote signals or barrier semaphores. Data moves between devices by JAX's collectives and lax.ppermute only.
A program may use at most 64 MiB of HBM per device.

v0:
```python
import jax
import jax.numpy as jnp
from jax import lax
from jax.sharding import PartitionSpec as P

NFRAC = 16
NPSF = 8
PSF_RADIUS = 4
PASSES = 16
HALO = 11
sentinel = 1000000.0
half_sentinel = 500000.0
pivot_span = 16.0


def _grid_pairs(nrow, ncol, dr, dc, flat):
    pairs = []
    for r in range(nrow):
        for c in range(ncol):
            tr, tc = (r - dr, c - dc)
            if 0 <= tr < nrow and 0 <= tc < ncol:
                pairs.append((flat(r, c), flat(tr, tc)))
    return pairs


def extended(block, row_dim, col_dim, width):
    nrow = lax.axis_size("row")
    ncol = lax.axis_size("col")
    rows = block.shape[row_dim]
    cols = block.shape[col_dim]

    def piece(dr, dc):
        part = block
        if dr == -1:
            part = lax.slice_in_dim(part, rows - width, rows, axis=row_dim)
        elif dr == 1:
            part = lax.slice_in_dim(part, 0, width, axis=row_dim)
        if dc == -1:
            part = lax.slice_in_dim(part, cols - width, cols, axis=col_dim)
        elif dc == 1:
            part = lax.slice_in_dim(part, 0, width, axis=col_dim)
        if dr == 0:
            pairs = _grid_pairs(1, ncol, 0, dc, lambda r, c: c)
            return lax.ppermute(part, "col", pairs)
        if dc == 0:
            pairs = _grid_pairs(nrow, 1, dr, 0, lambda r, c: r)
            return lax.ppermute(part, "row", pairs)
        pairs = _grid_pairs(nrow, ncol, dr, dc, lambda r, c: r * ncol + c)
        return lax.ppermute(part, ("row", "col"), pairs)

    bands = []
    for dr in (-1, 0, 1):
        line = [block if (dr, dc) == (0, 0) else piece(dr, dc) for dc in (-1, 0, 1)]
        bands.append(jnp.concatenate(line, axis=col_dim))
    return jnp.concatenate(bands, axis=row_dim)


def lanczos_table():
    fraction = jnp.arange(NFRAC, dtype=jnp.float32) / NFRAC
    offset_grid = jnp.arange(-2, 4, dtype=jnp.float32)
    spread = offset_grid[None, :] - fraction[:, None]
    kernel = jnp.sinc(spread) * jnp.sinc(spread / 3.0)
    return kernel / jnp.sum(kernel, axis=1, keepdims=True)


def blur_table():
    offset_grid = jnp.arange(-PSF_RADIUS, PSF_RADIUS + 1, dtype=jnp.float32)
    widths = 0.7 + 0.2 * jnp.arange(NPSF, dtype=jnp.float32)
    kernel = jnp.exp(-0.5 * (offset_grid[None, :] / widths[:, None]) ** 2)
    return kernel / jnp.sum(kernel, axis=1, keepdims=True)


def lookup(indices, entries, kernel_table):
    chooser = (indices[:, None] == lax.broadcasted_iota(jnp.int32, (1, entries), 1)).astype(
        jnp.float32
    )
    return jnp.dot(chooser, kernel_table, precision=lax.Precision.HIGHEST)


def placed_taps(weights, shifts):
    reach = 2 * HALO + 1
    positions = lax.broadcasted_iota(jnp.int32, (1, 1, reach), 2)
    tap_slot = HALO + shifts[:, None, None] + lax.broadcasted_iota(jnp.int32, (1, 6, 1), 1) - 2
    spread = (tap_slot == positions).astype(jnp.float32)
    return jnp.sum(weights[:, :, None] * spread, axis=1)


def resample_axis(stack, coefficients, out_len, which_axis):
    out_shape = list(stack.shape)
    out_shape[which_axis] = out_len
    total = jnp.zeros(tuple(out_shape), jnp.float32)
    for position in range(2 * HALO + 1):
        window = lax.slice_in_dim(stack, position, position + out_len, 1, which_axis)
        total = total + coefficients[:, position, None, None] * window
    return total


def bisect_lower(valid_count, count_below):

    def one_pass(sweep_no, bounds):
        lower_edge, upper_edge = bounds
        middle = 0.5 * (lower_edge + upper_edge)
        enough = 2.0 * count_below(middle) >= valid_count
        return (jnp.where(enough, lower_edge, middle), jnp.where(enough, middle, upper_edge))

    initial = (
        jnp.full(valid_count.shape, -pivot_span, jnp.float32),
        jnp.full(valid_count.shape, pivot_span, jnp.float32),
    )
    return lax.fori_loop(0, PASSES, one_pass, initial)[0]


def stack_median(pixel_stack):
    valid_count = jnp.sum(pixel_stack < half_sentinel, axis=0, dtype=jnp.float32)

    def count_below(middle):
        return jnp.sum(pixel_stack <= middle[None], axis=0, dtype=jnp.float32)

    lower_edge = bisect_lower(valid_count, count_below)
    return jnp.min(jnp.where(pixel_stack > lower_edge[None], pixel_stack, sentinel), axis=0)


def body(exposures, bad_pixels, offsets, warp_index, blur_index):
    group_size, row_count, col_count = exposures.shape
    kernel_table = lanczos_table()
    coef_down = placed_taps(lookup(warp_index[:, 0], NFRAC, kernel_table), offsets[:, 0])
    coef_across = placed_taps(lookup(warp_index[:, 1], NFRAC, kernel_table), offsets[:, 1])
    padded = extended(exposures, 1, 2, HALO)
    across = resample_axis(padded, coef_down, row_count, 1)
    warped = resample_axis(across, coef_across, col_count, 2)
    flagged = jnp.where(bad_pixels == 1, sentinel, warped)
    band = stack_median(lax.all_to_all(flagged, "exp", split_axis=1, concat_axis=0, tiled=True))
    groups = lax.axis_size("exp")
    median_sky = lax.all_to_all(
        jnp.tile(band, (groups, 1)), "exp", split_axis=0, concat_axis=0, tiled=True
    )
    bordered = extended(median_sky, 0, 1, PSF_RADIUS)
    blur = blur_table()
    taps = 2 * PSF_RADIUS + 1
    blurred_rows = jnp.zeros((NPSF, row_count, col_count + 2 * PSF_RADIUS), jnp.float32)
    for tap_no in range(taps):
        blurred_rows = (
            blurred_rows
            + blur[:, tap_no, None, None] * bordered[None, tap_no : tap_no + row_count, :]
        )
    smoothed = jnp.zeros((NPSF, row_count, col_count), jnp.float32)
    for tap_no in range(taps):
        smoothed = (
            smoothed + blur[:, tap_no, None, None] * blurred_rows[:, :, tap_no : tap_no + col_count]
        )
    chooser = (blur_index[:, None] == lax.broadcasted_iota(jnp.int32, (1, NPSF), 1)).astype(
        jnp.float32
    )
    sky_model = jnp.zeros((group_size, row_count, col_count), jnp.float32)
    for kernel_no in range(NPSF):
        sky_model = sky_model + chooser[:, kernel_no, None, None] * smoothed[kernel_no][None]
    residual = jnp.where(bad_pixels == 1, 0.0, warped - sky_model)
    return (residual, median_sky)


def solution(mesh):
    return jax.shard_map(
        body,
        mesh=mesh,
        in_specs=(
            P("exp", "row", "col"),
            P("exp", "row", "col"),
            P("exp", None),
            P("exp", None),
            P("exp"),
        ),
        out_specs=(P("exp", "row", "col"), P("row", "col")),
        check_vma=False,
    )
```

profile of v0, /device:TPU:1, one launch (start us, length us, event | category | flops | bytes accessed | tf_op | source)
XLA Modules:
  0.0 119.1 jit_solution(8014442783377771152)
XLA Ops:
  0.6 1.8 %copy.37 = f32[16,32,512]{2,0,1:T(8,128)S(1)} copy(f32[16,32,512]{2,1,0:T(8,128)} %param.8) | data formatting | bytes 2097152 | tf_op args[0]
  2.6 5.6 %collective-permute-start = (f32[16,11,11]{2,0,1:T(8,128)S(1)}, f32[16,11,11]{2,0,1:T(8,128)S(1)}, u32[]{:S(2)}, u32[]{:S(2)}) collective-permute-start(f32[16,11,11]{2,0,1:T(8,128)S(1)} %get-tuple-element.118), channel_id=1, source_target_pairs={{0,3},{2,5},{4,7},{8,11},{10,13},{12,15},{16,19},{18,21},{20,23},{... | collective-permute-start | bytes 23240 | tf_op jit(solution)/shard_map/ppermute | solution.py:49
  8.2 1.3 %collective-permute-start.2 = (f32[16,11,11]{2,0,1:T(8,128)S(1)}, f32[16,11,11]{2,0,1:T(8,128)S(1)}, u32[]{:S(2)}, u32[]{:S(2)}) collective-permute-start(f32[16,11,11]{2,0,1:T(8,128)S(1)} %get-tuple-element.121), channel_id=1, source_target_pairs={{1,2},{3,4},{5,6},{9,10},{11,12},{13,14},{17,18},{19,20},{21,22},{... | collective-permute-start | bytes 23240 | tf_op jit(solution)/shard_map/ppermute | solution.py:49
  9.5 4.3 %collective-permute-start.5 = (f32[16,11,11]{2,0,1:T(8,128)S(1)}, f32[16,11,11]{2,0,1:T(8,128)S(1)}, u32[]{:S(2)}, u32[]{:S(2)}) collective-permute-start(f32[16,11,11]{2,0,1:T(8,128)S(1)} %get-tuple-element.120), channel_id=1, source_target_pairs={{2,1},{4,3},{6,5},{10,9},{12,11},{14,13},{18,17},{20,19},{22,21},{... | collective-permute-start | bytes 23240 | tf_op jit(solution)/shard_map/ppermute | solution.py:49
  13.8 2.8 %collective-permute-start.1 = (f32[16,11,512]{2,0,1:T(8,128)S(1)}, f32[16,11,512]{2,0,1:T(8,128)S(1)}, u32[]{:S(2)}, u32[]{:S(2)}) collective-permute-start(f32[16,11,512]{2,0,1:T(8,128)S(1)} %get-tuple-element.122), channel_id=1, source_target_pairs={{0,2},{2,4},{4,6},{1,3},{3,5},{5,7},{8,10},{10,12},{12,14},{9,11},... | collective-permute-start | bytes 1081352 | tf_op jit(solution)/shard_map/ppermute | solution.py:47
  16.7 1.9 %collective-permute-start.6 = (f32[16,11,512]{2,0,1:T(8,128)S(1)}, f32[16,11,512]{2,0,1:T(8,128)S(1)}, u32[]{:S(2)}, u32[]{:S(2)}) collective-permute-start(f32[16,11,512]{2,0,1:T(8,128)S(1)} %get-tuple-element.123), channel_id=1, source_target_pairs={{2,0},{4,2},{6,4},{3,1},{5,3},{7,5},{10,8},{12,10},{14,12},{11,9},... | collective-permute-start | bytes 1081352 | tf_op jit(solution)/shard_map/ppermute | solution.py:47
  22.1 2.9 %collective-permute-start.3 = (f32[16,32,11]{2,0,1:T(8,128)S(1)}, f32[16,32,11]{2,0,1:T(8,128)S(1)}, u32[]{:S(2)}, u32[]{:S(2)}) collective-permute-start(f32[16,32,11]{2,0,1:T(8,128)S(1)} %get-tuple-element.124), channel_id=1, source_target_pairs={{0,1},{2,3},{4,5},{6,7},{8,9},{10,11},{12,13},{14,15},{16,17},{18,... | collective-permute-start | bytes 67592 | tf_op jit(solution)/shard_map/ppermute | solution.py:44
  25.0 1.3 %collective-permute-start.4 = (f32[16,32,11]{2,0,1:T(8,128)S(1)}, f32[16,32,11]{2,0,1:T(8,128)S(1)}, u32[]{:S(2)}, u32[]{:S(2)}) collective-permute-start(f32[16,32,11]{2,0,1:T(8,128)S(1)} %get-tuple-element.125), channel_id=1, source_target_pairs={{1,0},{3,2},{5,4},{7,6},{9,8},{11,10},{13,12},{15,14},{17,16},{19,... | collective-permute-start | bytes 67592 | tf_op jit(solution)/shard_map/ppermute | solution.py:44
  26.5 2.0 %collective-permute-done.7 = f32[16,11,11]{2,0,1:T(8,128)S(1)} collective-permute-done((f32[16,11,11]{2,0,1:T(8,128)S(1)}, f32[16,11,11]{2,0,1:T(8,128)S(1)}, u32[]{:S(2)}, u32[]{:S(2)}) %collective-permute-start.7) | collective-permute-done | bytes 7776 | tf_op jit(solution)/shard_map/ppermute | solution.py:49
  28.7 4.1 %collective-permute-done.4 = f32[16,32,11]{2,0,1:T(8,128)S(1)} collective-permute-done((f32[16,32,11]{2,0,1:T(8,128)S(1)}, f32[16,32,11]{2,0,1:T(8,128)S(1)}, u32[]{:S(2)}, u32[]{:S(2)}) %collective-permute-start.4) | collective-permute-done | bytes 22560 | tf_op jit(solution)/shard_map/ppermute | solution.py:44
  34.0 3.3 %fusion = f32[16,32,534]{2,0,1:T(8,128)S(1)} fusion(f32[16,43,534]{2,0,1:T(8,128)S(1)} %get-tuple-element.117, f32[16,43,534]{2,0,1:T(8,128)S(1)} %get-tuple-element.116, f32[16,32,11]{2,0,1:T(8,128)S(1)} %collective-permute-done.4, f32[16,32,512]{2,0,1:T(8,128)S(1)} %copy.37, f32[16,32,11]{2,0,1:T(8,128)S(1)} %collective-permute-done.3, ...), kind=kLoop, calls=%fused_computation.9 | loop fusion | flops 12850176 | bytes 26248640 | tf_op jit(solution)/shard_map/add | solution.py:94
  37.3 7.0 %broadcast_select_fusion = (f32[16,32,512]{2,0,1:T(8,128)}, f32[16,32,512]{2,0,1:T(8,128)S(1)}, pred[16,32,512]{2,0,1:T(8,128)(4,1)S(1)}) fusion(f32[16,32,534]{2,0,1:T(8,128)S(1)} %fusion, f32[16]{0:T(128)S(1)} %get-tuple-element.56, f32[16]{0:T(128)S(1)} %get-tuple-element.57, f32[16]{0:T(128)S(1)} %get-tuple-element.58, f32[16]{0:T(128)S(1)} %get-tuple-element.59, ...), kind=kLoop, calls=%fused_computation.120 | loop fusion | flops 12320768 | bytes 27526592 | tf_op jit(solution)/shard_map/jit(_where)/select_n | solution.py:131
  44.3 4.7 %all-to-all-start = ((f32[16,32,512]{2,0,1:T(8,128)}), f32[16,32,512]{2,0,1:T(8,128)S(1)}, u32[]{:S(2)}, u32[]{:S(2)}) async-start(f32[16,32,512]{2,0,1:T(8,128)} %get-tuple-element.113), calls=%async_computation | async-start | bytes 2097152 | tf_op jit(solution)/shard_map/all_to_all | solution.py:132
  49.2 25.1 %all-to-all-done = f32[16,32,512]{2,0,1:T(8,128)S(1)} async-done(((f32[16,32,512]{2,0,1:T(8,128)}), f32[16,32,512]{2,0,1:T(8,128)S(1)}, u32[]{:S(2)}, u32[]{:S(2)}) %all-to-all-start) | async-done | bytes 1048608 | tf_op jit(solution)/shard_map/all_to_all | solution.py:132
  75.1 3.6 %while.13 = (s32[]{:T(128)}, f32[8,512]{1,0:T(8,128)S(1)}, f32[8,512]{1,0:T(8,128)S(1)}, f32[64,8,512]{2,1,0:T(8,128)S(1)}, f32[8,512]{1,0:T(8,128)S(1)}, /*index=5*/s32[]{:T(128)}, s32[]{:T(128)}) while((s32[]{:T(128)}, f32[8,512]{1,0:T(8,128)S(1)}, f32[8,512]{1,0:T(8,128)S(1)}, f32[64,8,512]{2,1,0:T(8,128)S(1)}, ...), condition=%wide.region_7.9_spmd.clone, body=%wide.region_5.8_spmd.clone.sunk | while | flops 1110019 | bytes 1302617 | solution.py:110
  79.5 3.3 %all-to-all-start.1 = ((f32[4,8,512]{2,1,0:T(8,128)}), f32[4,8,512]{2,1,0:T(8,128)S(1)}, u32[]{:S(2)}, u32[]{:S(2)}) async-start(f32[4,8,512]{2,1,0:T(8,128)} %tile.2), calls=%async_computation.1 | async-start | bytes 131072 | tf_op jit(solution)/shard_map/all_to_all | solution.py:134
  82.8 4.5 %all-to-all-done.1 = f32[4,8,512]{2,1,0:T(8,128)S(1)} async-done(((f32[4,8,512]{2,1,0:T(8,128)}), f32[4,8,512]{2,1,0:T(8,128)S(1)}, u32[]{:S(2)}, u32[]{:S(2)}) %all-to-all-start.1) | async-done | bytes 65568 | tf_op jit(solution)/shard_map/all_to_all | solution.py:134
  87.4 1.5 %collective-permute-start.11 = (f32[32,4]{1,0:T(8,128)S(1)}, f32[32,4]{1,0:T(8,128)S(1)}, u32[]{:S(2)}, u32[]{:S(2)}) collective-permute-start(f32[32,4]{1,0:T(8,128)S(1)} %get-tuple-element.150), channel_id=1, source_target_pairs={{0,1},{2,3},{4,5},{6,7},{8,9},{10,11},{12,13},{14,15},{16,17},{18,... | collective-permute-start | bytes 1544 | tf_op jit(solution)/shard_map/ppermute | solution.py:44
  90.3 2.9 %collective-permute-start.14 = (f32[4,512]{1,0:T(4,128)S(1)}, f32[4,512]{1,0:T(4,128)S(1)}, u32[]{:S(2)}, u32[]{:S(2)}) collective-permute-start(f32[4,512]{1,0:T(4,128)S(1)} %get-tuple-element.149), channel_id=1, source_target_pairs={{2,0},{4,2},{6,4},{3,1},{5,3},{7,5},{10,8},{12,10},{14,12},{11,9},... | collective-permute-start | bytes 24584 | tf_op jit(solution)/shard_map/ppermute | solution.py:47
  93.2 8.0 %collective-permute-start.9 = (f32[4,512]{1,0:T(4,128)S(1)}, f32[4,512]{1,0:T(4,128)S(1)}, u32[]{:S(2)}, u32[]{:S(2)}) collective-permute-start(f32[4,512]{1,0:T(4,128)S(1)} %get-tuple-element.148), channel_id=1, source_target_pairs={{0,2},{2,4},{4,6},{1,3},{3,5},{5,7},{8,10},{10,12},{12,14},{9,11},... | collective-permute-start | bytes 24584 | tf_op jit(solution)/shard_map/ppermute | solution.py:47
  101.2 1.3 %collective-permute-start.10 = (f32[4,4]{1,0:T(4,128)S(1)}, f32[4,4]{1,0:T(4,128)S(1)}, u32[]{:S(2)}, u32[]{:S(2)}) collective-permute-start(f32[4,4]{1,0:T(4,128)S(1)} %get-tuple-element.147), channel_id=1, source_target_pairs={{1,2},{3,4},{5,6},{9,10},{11,12},{13,14},{17,18},{19,20},{21,22},{... | collective-permute-start | bytes 200 | tf_op jit(solution)/shard_map/ppermute | solution.py:49
  102.5 4.3 %collective-permute-start.13 = (f32[4,4]{1,0:T(4,128)S(1)}, f32[4,4]{1,0:T(4,128)S(1)}, u32[]{:S(2)}, u32[]{:S(2)}) collective-permute-start(f32[4,4]{1,0:T(4,128)S(1)} %get-tuple-element.146), channel_id=1, source_target_pairs={{2,1},{4,3},{6,5},{10,9},{12,11},{14,13},{18,17},{20,19},{22,21},{... | collective-permute-start | bytes 200 | tf_op jit(solution)/shard_map/ppermute | solution.py:49
  108.2 5.3 %collective-permute-start.8 = (f32[4,4]{1,0:T(4,128)S(1)}, f32[4,4]{1,0:T(4,128)S(1)}, u32[]{:S(2)}, u32[]{:S(2)}) collective-permute-start(f32[4,4]{1,0:T(4,128)S(1)} %get-tuple-element.144), channel_id=1, source_target_pairs={{0,3},{2,5},{4,7},{8,11},{10,13},{12,15},{16,19},{18,21},{20,23},{... | collective-permute-start | bytes 200 | tf_op jit(solution)/shard_map/ppermute | solution.py:49
  116.9 1.6 %copy.47 = f32[16,32,512]{2,1,0:T(8,128)} copy(f32[16,32,512]{2,0,1:T(8,128)S(1)} %subtract_select_fusion) | data formatting | bytes 2097152
  (148 shorter events, 16.6 us)
Async XLA Ops:
  2.6 16.2 %copy-start.1 = (s32[16,2]{0,1:T(2,128)S(1)}, s32[16,2]{0,1:T(2,128)}, u32[]{:S(2)}) copy-start(s32[16,2]{0,1:T(2,128)} %param.11) | copy-start | bytes 388
  2.6 16.2 %copy-start.2 = (s32[16,2]{0,1:T(2,128)S(1)}, s32[16,2]{0,1:T(2,128)}, u32[]{:S(2)}) copy-start(s32[16,2]{0,1:T(2,128)} %param.10) | copy-start | bytes 388
  2.6 18.2 %collective-permute-start = (f32[16,11,11]{2,0,1:T(8,128)S(1)}, f32[16,11,11]{2,0,1:T(8,128)S(1)}, u32[]{:S(2)}, u32[]{:S(2)}) collective-permute-start(f32[16,11,11]{2,0,1:T(8,128)S(1)} %get-tuple-element.118), channel_id=1, source_target_pairs={{0,3},{2,5},{4,7},{8,11},{10,13},{12,15},{16,19},{18,21},{20,23},{... | collective-permute-start | bytes 23240 | tf_op jit(solution)/shard_map/ppermute | solution.py:49
  8.2 13.9 %collective-permute-start.2 = (f32[16,11,11]{2,0,1:T(8,128)S(1)}, f32[16,11,11]{2,0,1:T(8,128)S(1)}, u32[]{:S(2)}, u32[]{:S(2)}) collective-permute-start(f32[16,11,11]{2,0,1:T(8,128)S(1)} %get-tuple-element.121), channel_id=1, source_target_pairs={{1,2},{3,4},{5,6},{9,10},{11,12},{13,14},{17,18},{19,20},{21,22},{... | collective-permute-start | bytes 23240 | tf_op jit(solution)/shard_map/ppermute | solution.py:49
  9.5 15.5 %collective-permute-start.5 = (f32[16,11,11]{2,0,1:T(8,128)S(1)}, f32[16,11,11]{2,0,1:T(8,128)S(1)}, u32[]{:S(2)}, u32[]{:S(2)}) collective-permute-start(f32[16,11,11]{2,0,1:T(8,128)S(1)} %get-tuple-element.120), channel_id=1, source_target_pairs={{2,1},{4,3},{6,5},{10,9},{12,11},{14,13},{18,17},{20,19},{22,21},{... | collective-permute-start | bytes 23240 | tf_op jit(solution)/shard_map/ppermute | solution.py:49
  13.8 18.9 %collective-permute-start.1 = (f32[16,11,512]{2,0,1:T(8,128)S(1)}, f32[16,11,512]{2,0,1:T(8,128)S(1)}, u32[]{:S(2)}, u32[]{:S(2)}) collective-permute-start(f32[16,11,512]{2,0,1:T(8,128)S(1)} %get-tuple-element.122), channel_id=1, source_target_pairs={{0,2},{2,4},{4,6},{1,3},{3,5},{5,7},{8,10},{10,12},{12,14},{9,11},... | collective-permute-start | bytes 1081352 | tf_op jit(solution)/shard_map/ppermute | solution.py:47
  16.7 16.1 %collective-permute-start.6 = (f32[16,11,512]{2,0,1:T(8,128)S(1)}, f32[16,11,512]{2,0,1:T(8,128)S(1)}, u32[]{:S(2)}, u32[]{:S(2)}) collective-permute-start(f32[16,11,512]{2,0,1:T(8,128)S(1)} %get-tuple-element.123), channel_id=1, source_target_pairs={{2,0},{4,2},{6,4},{3,1},{5,3},{7,5},{10,8},{12,10},{14,12},{11,9},... | collective-permute-start | bytes 1081352 | tf_op jit(solution)/shard_map/ppermute | solution.py:47
  20.8 7.7 %collective-permute-start.7 = (f32[16,11,11]{2,0,1:T(8,128)S(1)}, f32[16,11,11]{2,0,1:T(8,128)S(1)}, u32[]{:S(2)}, u32[]{:S(2)}) collective-permute-start(f32[16,11,11]{2,0,1:T(8,128)S(1)} %get-tuple-element.119), channel_id=1, source_target_pairs={{3,0},{5,2},{7,4},{11,8},{13,10},{15,12},{19,16},{21,18},{23,20},{... | collective-permute-start | bytes 23240 | tf_op jit(solution)/shard_map/ppermute | solution.py:49
  22.1 6.6 %collective-permute-start.3 = (f32[16,32,11]{2,0,1:T(8,128)S(1)}, f32[16,32,11]{2,0,1:T(8,128)S(1)}, u32[]{:S(2)}, u32[]{:S(2)}) collective-permute-start(f32[16,32,11]{2,0,1:T(8,128)S(1)} %get-tuple-element.124), channel_id=1, source_target_pairs={{0,1},{2,3},{4,5},{6,7},{8,9},{10,11},{12,13},{14,15},{16,17},{18,... | collective-permute-start | bytes 67592 | tf_op jit(solution)/shard_map/ppermute | solution.py:44
  25.0 7.8 %collective-permute-start.4 = (f32[16,32,11]{2,0,1:T(8,128)S(1)}, f32[16,32,11]{2,0,1:T(8,128)S(1)}, u32[]{:S(2)}, u32[]{:S(2)}) collective-permute-start(f32[16,32,11]{2,0,1:T(8,128)S(1)} %get-tuple-element.125), channel_id=1, source_target_pairs={{1,0},{3,2},{5,4},{7,6},{9,8},{11,10},{13,12},{15,14},{17,16},{19,... | collective-permute-start | bytes 67592 | tf_op jit(solution)/shard_map/ppermute | solution.py:44
  33.9 3.3 %copy-start = (s32[16,32,512]{2,1,0:T(8,128)S(1)}, s32[16,32,512]{2,1,0:T(8,128)}, u32[]{:S(2)}) copy-start(s32[16,32,512]{2,1,0:T(8,128)} %param.9) | copy-start | bytes 3145732
  44.3 4.8 %copy-start.3 = (s32[16]{0:T(128)S(1)}, s32[16]{0:T(128)}, u32[]{:S(2)}) copy-start(s32[16]{0:T(128)} %param.12) | copy-start | bytes 196
  44.3 30.0 %all-to-all-start = ((f32[16,32,512]{2,0,1:T(8,128)}), f32[16,32,512]{2,0,1:T(8,128)S(1)}, u32[]{:S(2)}, u32[]{:S(2)}) async-start(f32[16,32,512]{2,0,1:T(8,128)} %get-tuple-element.113), calls=%async_computation | async-start | bytes 2097152 | tf_op jit(solution)/shard_map/all_to_all | solution.py:132
  79.5 7.9 %all-to-all-start.1 = ((f32[4,8,512]{2,1,0:T(8,128)}), f32[4,8,512]{2,1,0:T(8,128)S(1)}, u32[]{:S(2)}, u32[]{:S(2)}) async-start(f32[4,8,512]{2,1,0:T(8,128)} %tile.2), calls=%async_computation.1 | async-start | bytes 131072 | tf_op jit(solution)/shard_map/all_to_all | solution.py:134
  87.4 15.1 %collective-permute-start.11 = (f32[32,4]{1,0:T(8,128)S(1)}, f32[32,4]{1,0:T(8,128)S(1)}, u32[]{:S(2)}, u32[]{:S(2)}) collective-permute-start(f32[32,4]{1,0:T(8,128)S(1)} %get-tuple-element.150), channel_id=1, source_target_pairs={{0,1},{2,3},{4,5},{6,7},{8,9},{10,11},{12,13},{14,15},{16,17},{18,... | collective-permute-start | bytes 1544 | tf_op jit(solution)/shard_map/ppermute | solution.py:44
  89.0 17.8 %collective-permute-start.12 = (f32[32,4]{1,0:T(8,128)S(1)}, f32[32,4]{1,0:T(8,128)S(1)}, u32[]{:S(2)}, u32[]{:S(2)}) collective-permute-start(f32[32,4]{1,0:T(8,128)S(1)} %get-tuple-element.151), channel_id=1, source_target_pairs={{1,0},{3,2},{5,4},{7,6},{9,8},{11,10},{13,12},{15,14},{17,16},{19,... | collective-permute-start | bytes 1544 | tf_op jit(solution)/shard_map/ppermute | solution.py:44
  90.3 23.8 %collective-permute-start.14 = (f32[4,512]{1,0:T(4,128)S(1)}, f32[4,512]{1,0:T(4,128)S(1)}, u32[]{:S(2)}, u32[]{:S(2)}) collective-permute-start(f32[4,512]{1,0:T(4,128)S(1)} %get-tuple-element.149), channel_id=1, source_target_pairs={{2,0},{4,2},{6,4},{3,1},{5,3},{7,5},{10,8},{12,10},{14,12},{11,9},... | collective-permute-start | bytes 24584 | tf_op jit(solution)/shard_map/ppermute | solution.py:47
  93.2 20.9 %collective-permute-start.9 = (f32[4,512]{1,0:T(4,128)S(1)}, f32[4,512]{1,0:T(4,128)S(1)}, u32[]{:S(2)}, u32[]{:S(2)}) collective-permute-start(f32[4,512]{1,0:T(4,128)S(1)} %get-tuple-element.148), channel_id=1, source_target_pairs={{0,2},{2,4},{4,6},{1,3},{3,5},{5,7},{8,10},{10,12},{12,14},{9,11},... | collective-permute-start | bytes 24584 | tf_op jit(solution)/shard_map/ppermute | solution.py:47
  101.2 7.0 %collective-permute-start.10 = (f32[4,4]{1,0:T(4,128)S(1)}, f32[4,4]{1,0:T(4,128)S(1)}, u32[]{:S(2)}, u32[]{:S(2)}) collective-permute-start(f32[4,4]{1,0:T(4,128)S(1)} %get-tuple-element.147), channel_id=1, source_target_pairs={{1,2},{3,4},{5,6},{9,10},{11,12},{13,14},{17,18},{19,20},{21,22},{... | collective-permute-start | bytes 200 | tf_op jit(solution)/shard_map/ppermute | solution.py:49
  102.5 11.0 %collective-permute-start.13 = (f32[4,4]{1,0:T(4,128)S(1)}, f32[4,4]{1,0:T(4,128)S(1)}, u32[]{:S(2)}, u32[]{:S(2)}) collective-permute-start(f32[4,4]{1,0:T(4,128)S(1)} %get-tuple-element.146), channel_id=1, source_target_pairs={{2,1},{4,3},{6,5},{10,9},{12,11},{14,13},{18,17},{20,19},{22,21},{... | collective-permute-start | bytes 200 | tf_op jit(solution)/shard_map/ppermute | solution.py:49
  106.8 6.8 %collective-permute-start.15 = (f32[4,4]{1,0:T(4,128)S(1)}, f32[4,4]{1,0:T(4,128)S(1)}, u32[]{:S(2)}, u32[]{:S(2)}) collective-permute-start(f32[4,4]{1,0:T(4,128)S(1)} %get-tuple-element.145), channel_id=1, source_target_pairs={{3,0},{5,2},{7,4},{11,8},{13,10},{15,12},{19,16},{21,18},{23,20},{... | collective-permute-start | bytes 200 | tf_op jit(solution)/shard_map/ppermute | solution.py:49
  108.2 5.9 %collective-permute-start.8 = (f32[4,4]{1,0:T(4,128)S(1)}, f32[4,4]{1,0:T(4,128)S(1)}, u32[]{:S(2)}, u32[]{:S(2)}) collective-permute-start(f32[4,4]{1,0:T(4,128)S(1)} %get-tuple-element.144), channel_id=1, source_target_pairs={{0,3},{2,5},{4,7},{8,11},{10,13},{12,15},{16,19},{18,21},{20,23},{... | collective-permute-start | bytes 200 | tf_op jit(solution)/shard_map/ppermute | solution.py:49
where the time goes:
time: 120 us; the launch traced here: 119 us
  starting transfers between devices  55.2 us (46%)
  waiting for transfers between devices  36.5 us (30%)
  other arithmetic  17.9 us (15%)
  local copies, waits for them, and re-layouts  7.33 us (6%)
    all_to_all x1, waiting for transfers between devices, body(): lax.all_to_all(flagged, 'exp', split_axis=1, concat_axis=0, tiled=True)  25.1 us
    ppermute x8, starting transfers between devices, piece(): return lax.ppermute(part, ('row', 'col'), pairs)  24.6 us
    ppermute x4, starting transfers between devices, piece(): return lax.ppermute(part, 'row', pairs)  15.6 us
    select_n x1, other arithmetic, body(): flagged = jnp.where(bad_pixels == 1, sentinel, warped)  6.99 us
    ppermute x4, starting transfers between devices, piece(): return lax.ppermute(part, 'col', pairs)  6.92 us
    all_to_all x1, starting transfers between devices, body(): lax.all_to_all(flagged, 'exp', split_axis=1, concat_axis=0, tiled=True)  4.72 us
    all_to_all x1, waiting for transfers between devices, body(): lax.all_to_all(jnp.tile(band, (groups, 1)), 'exp', split_axis=0, concat_a...  4.55 us
    ppermute x4, waiting for transfers between devices, piece(): return lax.ppermute(part, 'col', pairs)  4.33 us
  transfers between devices with their start and end apart: 18, of which 6 were waited for; matrix products, arithmetic and copies ran while one was open for 2% of the time, Pallas kernels for 0%

commit v1 on v0

--- a/solution.py
+++ b/solution.py
@@ -11,6 +11,28 @@
 sentinel = 1000000.0
 half_sentinel = 500000.0
 pivot_span = 16.0
+
+
+def split_up(array, dim, size):
+    before, after = (array.shape[:dim], array.shape[dim + 1 :])
+    return jnp.moveaxis(array.reshape(*before, size, -1, *after), dim, 0)
+
+
+def laid_out(blocks, dim):
+    lengths = list(blocks.shape[1:])
+    lengths[dim] *= blocks.shape[0]
+    return jnp.moveaxis(blocks, 0, dim).reshape(lengths)
+
+
+def swapped_with_each(x, axis, split_dim, concat_dim):
+    count, here = (lax.axis_size(axis), lax.axis_index(axis))
+    blocks = split_up(x, split_dim, count)
+    outs = [blocks[here]]
+    for step in range(1, count):
+        sent = blocks[here ^ step]
+        outs.append(lax.ppermute(sent, axis, [(i, i ^ step) for i in range(count)]))
+    blocks = jnp.stack(outs)[here ^ jnp.arange(count)]
+    return laid_out(blocks, concat_dim)
 
 
 def _grid_pairs(nrow, ncol, dr, dc, flat):
@@ -129,7 +151,7 @@
     across = resample_axis(padded, coef_down, row_count, 1)
     warped = resample_axis(across, coef_across, col_count, 2)
     flagged = jnp.where(bad_pixels == 1, sentinel, warped)
-    band = stack_median(lax.all_to_all(flagged, "exp", split_axis=1, concat_axis=0, tiled=True))
+    band = stack_median(swapped_with_each(flagged, "exp", 1, 0))
     groups = lax.axis_size("exp")
     median_sky = lax.all_to_all(
         jnp.tile(band, (groups, 1)), "exp", split_axis=0, concat_axis=0, tiled=True

time: 120 us -> 126 us (1.050)
  the two profiles are of different devices: /device:TPU:1 before, /device:TPU:3 now
where the time goes in v1:
time: 126 us; the launch traced here: 125 us
  starting transfers between devices  44.9 us (36%)
  waiting for transfers between devices  40.3 us (32%)
  other arithmetic  26 us (21%)
  local copies, waits for them, and re-layouts  11.3 us (9%)
  between operations  1.68 us (1%)
    ppermute x8, starting transfers between devices, piece(): return lax.ppermute(part, ('row', 'col'), pairs)  24.8 us
    ppermute x3, waiting for transfers between devices, swapped_with_each(): outs.append(lax.ppermute(sent, axis, [(i, i ^ step) for i in range(count)]))  20.7 us
    ppermute x8, waiting for transfers between devices, piece(): return lax.ppermute(part, ('row', 'col'), pairs)  14.6 us
    ppermute x4, starting transfers between devices, piece(): return lax.ppermute(part, 'row', pairs)  7.79 us
    reshape x1, other arithmetic, split_up(): return jnp.moveaxis(array.reshape(*before, size, -1, *after), dim, 0)  7.55 us
    add x1, other arithmetic, resample_axis(): total = total + coefficients[:, position, None, None] * window  5.85 us
    ppermute x4, starting transfers between devices, piece(): return lax.ppermute(part, 'col', pairs)  5.14 us
    all_to_all x1, waiting for transfers between devices, body(): lax.all_to_all(jnp.tile(band, (groups, 1)), 'exp', split_axis=0, concat_a...  5 us
  transfers between devices with their start and end apart: 20, of which 5 were waited for; matrix products, arithmetic and copies ran while one was open for 6% of the time, Pallas kernels for 0%

profile of v1, /device:TPU:3, one launch (start us, length us, event | category | flops | bytes accessed | tf_op | source)
XLA Modules:
  0.0 125.3 jit_solution(16536986357728254833)
XLA Ops:
  0.6 2.0 %fusion.132 = (f32[16,11,11]{2,1,0:T(8,128)S(1)}, f32[16,11,11]{2,1,0:T(8,128)}, f32[16,11,11]{2,1,0:T(8,128)S(1)}, f32[16,11,11]{2,1,0:T(8,128)}) fusion(f32[16,32,512]{2,1,0:T(8,128)} %param.8), kind=kLoop, calls=%fused_computation.314 | loop fusion | bytes 61952 | tf_op jit(solution)/shard_map/slice | solution.py:61
  2.6 3.8 %collective-permute-start.2 = (f32[16,11,11]{2,1,0:T(8,128)S(1)}, f32[16,11,11]{2,1,0:T(8,128)S(1)}, u32[]{:S(2)}, u32[]{:S(2)}) collective-permute-start(f32[16,11,11]{2,1,0:T(8,128)S(1)} %get-tuple-element.118), channel_id=1, source_target_pairs={{1,2},{3,4},{5,6},{9,10},{11,12},{13,14},{17,18},{19,20},{21,22},{... | collective-permute-start | bytes 23240 | tf_op jit(solution)/shard_map/ppermute | solution.py:71
  7.4 2.0 %collective-permute-start.1 = (f32[16,11,512]{2,1,0:T(8,128)}, f32[16,11,512]{2,1,0:T(8,128)S(1)}, u32[]{:S(2)}, u32[]{:S(2)}) collective-permute-start(f32[16,11,512]{2,1,0:T(8,128)} %get-tuple-element.120), channel_id=1, source_target_pairs={{0,2},{2,4},{4,6},{1,3},{3,5},{5,7},{8,10},{10,12},{12,14},{9,11},... | collective-permute-start | bytes 1081352 | tf_op jit(solution)/shard_map/ppermute | solution.py:69
  10.7 4.9 %collective-permute-start.7 = (f32[16,11,11]{2,1,0:T(8,128)}, f32[16,11,11]{2,1,0:T(8,128)}, u32[]{:S(2)}, u32[]{:S(2)}) collective-permute-start(f32[16,11,11]{2,1,0:T(8,128)} %get-tuple-element.119), channel_id=1, source_target_pairs={{3,0},{5,2},{7,4},{11,8},{13,10},{15,12},{19,16},{21,18},{23,20},{... | collective-permute-start | bytes 23240 | tf_op jit(solution)/shard_map/ppermute | solution.py:71
  15.6 1.9 %collective-permute-start.6 = (f32[16,11,512]{2,1,0:T(8,128)S(1)}, f32[16,11,512]{2,1,0:T(8,128)S(1)}, u32[]{:S(2)}, u32[]{:S(2)}) collective-permute-start(f32[16,11,512]{2,1,0:T(8,128)S(1)} %get-tuple-element.121), channel_id=1, source_target_pairs={{2,0},{4,2},{6,4},{3,1},{5,3},{7,5},{10,8},{12,10},{14,12},{11,9},... | collective-permute-start | bytes 1081352 | tf_op jit(solution)/shard_map/ppermute | solution.py:69
  23.1 1.3 %collective-permute-start.4 = (f32[16,32,11]{2,1,0:T(8,128)}, f32[16,32,11]{2,1,0:T(8,128)S(1)}, u32[]{:S(2)}, u32[]{:S(2)}) collective-permute-start(f32[16,32,11]{2,1,0:T(8,128)} %get-tuple-element.123), channel_id=1, source_target_pairs={{1,0},{3,2},{5,4},{7,6},{9,8},{11,10},{13,12},{15,14},{17,16},{19,... | collective-permute-start | bytes 67592 | tf_op jit(solution)/shard_map/ppermute | solution.py:66
  28.4 10.3 %collective-permute-done.5 = f32[16,11,11]{2,1,0:T(8,128)} collective-permute-done((f32[16,11,11]{2,1,0:T(8,128)}, f32[16,11,11]{2,1,0:T(8,128)}, u32[]{:S(2)}, u32[]{:S(2)}) %collective-permute-start.5) | collective-permute-done | bytes 7776 | tf_op jit(solution)/shard_map/ppermute | solution.py:71
  38.6 3.3 %maximum_maximum_fusion = (f32[16,43,534]{2,1,0:T(8,128)S(1)}, f32[16,43,534]{2,1,0:T(8,128)S(1)}) fusion(f32[16,32,11]{2,1,0:T(8,128)S(1)} %collective-permute-done.4, f32[16,32,512]{2,1,0:T(8,128)S(1)} %copy-done, f32[16,32,11]{2,1,0:T(8,128)S(1)} %collective-permute-done.3, f32[16,11,11]{2,1,0:T(8,128)S(1)} %collective-permute-done.2, ...), kind=kLoop, calls=%fused_computation.7 | loop fusion | flops 3673920 | bytes 4784640 | tf_op jit(solution)/shard_map/concatenate | solution.py:77
  42.3 5.9 %fusion = f32[16,32,534]{2,1,0:T(8,128)S(1)} fusion(f32[16,43,534]{2,1,0:T(8,128)S(1)} %get-tuple-element.111, f32[16,43,534]{2,1,0:T(8,128)S(1)} %get-tuple-element.110, f32[16,32,11]{2,1,0:T(8,128)S(1)} %collective-permute-done.4, f32[16,32,512]{2,1,0:T(8,128)S(1)} %copy-done, f32[16,32,11]{2,1,0:T(8,128)S(1)} %collective-permute-done.3, ...), kind=kLoop, calls=%fused_computation.10 | loop fusion | flops 12850176 | bytes 26248640 | tf_op jit(solution)/shard_map/add | solution.py:116
  48.4 7.5 %select_bitcast_fusion = (f32[16,4,8,512]{3,2,1,0:T(8,128)S(1)}, f32[16,32,512]{2,1,0:T(8,128)S(1)}, pred[16,32,512]{2,1,0:T(8,128)(4,1)S(1)}) fusion(f32[16,32,534]{2,1,0:T(8,128)S(1)} %fusion, f32[16]{0:T(128)S(1)} %copy-done.6, f32[16]{0:T(128)S(1)} %copy-done.7, f32[16]{0:T(128)S(1)} %copy-done.8, f32[16]{0:T(128)S(1)} %copy-done.9, ...), kind=kLoop, calls=%fused_computation.103 | loop fusion | flops 12320768 | bytes 27526592 | tf_op jit(solution)/shard_map/reshape | solution.py:18
  56.1 3.4 %collective-permute-start.10 = (f32[16,8,512]{2,1,0:T(8,128)S(1)}, f32[16,8,512]{2,1,0:T(8,128)S(1)}, u32[]{:S(2)}, u32[]{:S(2)}) collective-permute-start(f32[16,8,512]{2,1,0:T(8,128)S(1)} %get-tuple-element.113), channel_id=1, source_target_pairs={{0,24},{8,16},{16,8},{24,0},{1,25},{9,17},{17,9},{25,1},{2,26},{10... | collective-permute-start | bytes 786440 | tf_op jit(solution)/shard_map/ppermute | solution.py:33
  59.9 6.3 %collective-permute-done.10 = f32[16,8,512]{2,1,0:T(8,128)S(1)} collective-permute-done((f32[16,8,512]{2,1,0:T(8,128)S(1)}, f32[16,8,512]{2,1,0:T(8,128)S(1)}, u32[]{:S(2)}, u32[]{:S(2)}) %collective-permute-start.10) | collective-permute-done | bytes 262176 | tf_op jit(solution)/shard_map/ppermute | solution.py:33
  66.1 14.5 %collective-permute-done.9 = f32[16,8,512]{2,1,0:T(8,128)S(1)} collective-permute-done((f32[16,8,512]{2,1,0:T(8,128)S(1)}, f32[16,8,512]{2,1,0:T(8,128)S(1)}, u32[]{:S(2)}, u32[]{:S(2)}) %collective-permute-start.9) | collective-permute-done | bytes 262176 | tf_op jit(solution)/shard_map/ppermute | solution.py:33
  83.3 3.6 %while.13 = (s32[]{:T(128)}, f32[8,512]{1,0:T(8,128)S(1)}, f32[8,512]{1,0:T(8,128)S(1)}, f32[64,8,512]{2,1,0:T(8,128)S(1)}, f32[8,512]{1,0:T(8,128)S(1)}, /*index=5*/s32[]{:T(128)}, s32[]{:T(128)}) while((s32[]{:T(128)}, f32[8,512]{1,0:T(8,128)S(1)}, f32[8,512]{1,0:T(8,128)S(1)}, f32[64,8,512]{2,1,0:T(8,128)S(1)}, ...), condition=%wide.region_7.9_spmd.clone, body=%wide.region_5.8_spmd.clone.sunk | while | flops 1110019 | bytes 1302625 | solution.py:132
  87.8 3.5 %all-to-all-start = ((f32[4,8,512]{2,1,0:T(8,128)}), f32[4,8,512]{2,1,0:T(8,128)S(1)}, u32[]{:S(2)}, u32[]{:S(2)}) async-start(f32[4,8,512]{2,1,0:T(8,128)} %tile.2), calls=%async_computation | async-start | bytes 131072 | tf_op jit(solution)/shard_map/all_to_all | solution.py:156
  91.2 5.0 %all-to-all-done = f32[4,8,512]{2,1,0:T(8,128)S(1)} async-done(((f32[4,8,512]{2,1,0:T(8,128)}), f32[4,8,512]{2,1,0:T(8,128)S(1)}, u32[]{:S(2)}, u32[]{:S(2)}) %all-to-all-start) | async-done | bytes 65568 | tf_op jit(solution)/shard_map/all_to_all | solution.py:156
  99.0 6.5 %collective-permute-start.13 = (f32[4,4]{1,0:T(4,128)S(1)}, f32[4,4]{1,0:T(4,128)S(1)}, u32[]{:S(2)}, u32[]{:S(2)}) collective-permute-start(f32[4,4]{1,0:T(4,128)S(1)} %get-tuple-element.145), channel_id=1, source_target_pairs={{1,2},{3,4},{5,6},{9,10},{11,12},{13,14},{17,18},{19,20},{21,22},{... | collective-permute-start | bytes 200 | tf_op jit(solution)/shard_map/ppermute | solution.py:71
  105.4 1.9 %collective-permute-start.12 = (f32[4,512]{1,0:T(4,128)S(1)}, f32[4,512]{1,0:T(4,128)S(1)}, u32[]{:S(2)}, u32[]{:S(2)}) collective-permute-start(f32[4,512]{1,0:T(4,128)S(1)} %get-tuple-element.146), channel_id=1, source_target_pairs={{0,2},{2,4},{4,6},{1,3},{3,5},{5,7},{8,10},{10,12},{12,14},{9,11},... | collective-permute-start | bytes 24584 | tf_op jit(solution)/shard_map/ppermute | solution.py:69
  107.4 1.3 %collective-permute-start.11 = (f32[4,4]{1,0:T(4,128)S(1)}, f32[4,4]{1,0:T(4,128)S(1)}, u32[]{:S(2)}, u32[]{:S(2)}) collective-permute-start(f32[4,4]{1,0:T(4,128)S(1)} %get-tuple-element.142), channel_id=1, source_target_pairs={{0,3},{2,5},{4,7},{8,11},{10,13},{12,15},{16,19},{18,21},{20,23},{... | collective-permute-start | bytes 200 | tf_op jit(solution)/shard_map/ppermute | solution.py:71
  108.7 4.3 %collective-permute-start.18 = (f32[4,4]{1,0:T(4,128)S(1)}, f32[4,4]{1,0:T(4,128)S(1)}, u32[]{:S(2)}, u32[]{:S(2)}) collective-permute-start(f32[4,4]{1,0:T(4,128)S(1)} %get-tuple-element.143), channel_id=1, source_target_pairs={{3,0},{5,2},{7,4},{11,8},{13,10},{15,12},{19,16},{21,18},{23,20},{... | collective-permute-start | bytes 200 | tf_op jit(solution)/shard_map/ppermute | solution.py:71
  112.9 1.9 %collective-permute-start.17 = (f32[4,512]{1,0:T(4,128)S(1)}, f32[4,512]{1,0:T(4,128)S(1)}, u32[]{:S(2)}, u32[]{:S(2)}) collective-permute-start(f32[4,512]{1,0:T(4,128)S(1)} %get-tuple-element.147), channel_id=1, source_target_pairs={{2,0},{4,2},{6,4},{3,1},{5,3},{7,5},{10,8},{12,10},{14,12},{11,9},... | collective-permute-start | bytes 24584 | tf_op jit(solution)/shard_map/ppermute | solution.py:69
  115.0 1.5 %collective-permute-start.16 = (f32[4,4]{1,0:T(4,128)S(1)}, f32[4,4]{1,0:T(4,128)S(1)}, u32[]{:S(2)}, u32[]{:S(2)}) collective-permute-start(f32[4,4]{1,0:T(4,128)S(1)} %get-tuple-element.144), channel_id=1, source_target_pairs={{2,1},{4,3},{6,5},{10,9},{12,11},{14,13},{18,17},{20,19},{22,21},{... | collective-permute-start | bytes 200 | tf_op jit(solution)/shard_map/ppermute | solution.py:71
  116.5 4.3 %collective-permute-done.16 = f32[4,4]{1,0:T(4,128)S(1)} collective-permute-done((f32[4,4]{1,0:T(4,128)S(1)}, f32[4,4]{1,0:T(4,128)S(1)}, u32[]{:S(2)}, u32[]{:S(2)}) %collective-permute-start.16) | collective-permute-done | bytes 96 | tf_op jit(solution)/shard_map/ppermute | solution.py:71
  122.9 1.8 %subtract_select_fusion = f32[16,32,512]{2,1,0:T(8,128)} fusion(pred[16,32,512]{2,1,0:T(8,128)(4,1)S(1)} %get-tuple-element.109, f32[16,32,512]{2,1,0:T(8,128)S(1)} %get-tuple-element.108, f32[32,512]{1,0:T(8,128)S(1)} %get-tuple-element.125, f32[16]{0:T(128)S(1)} %get-tuple-element.160, f32[32,512]{1,0:T(8,128)S(1)} %get-tuple-element.126, ...), kind=kLoop, calls=%fused_computation.101 | loop fusion | flops 4456448 | bytes 2884096 | tf_op jit(solution)/shard_map/jit(_where)/select_n | solution.py:179
  (244 shorter events, 24.0 us)
Async XLA Ops:
  2.6 15.8 %copy-start.45 = (s32[16,2]{0,1:T(2,128)S(1)}, s32[16,2]{0,1:T(2,128)}, u32[]{:S(2)}) copy-start(s32[16,2]{0,1:T(2,128)} %param.11) | copy-start | bytes 388
  2.6 15.8 %copy-start.46 = (s32[16,2]{0,1:T(2,128)S(1)}, s32[16,2]{0,1:T(2,128)}, u32[]{:S(2)}) copy-start(s32[16,2]{0,1:T(2,128)} %param.10) | copy-start | bytes 388
  2.6 20.5 %collective-permute-start.2 = (f32[16,11,11]{2,1,0:T(8,128)S(1)}, f32[16,11,11]{2,1,0:T(8,128)S(1)}, u32[]{:S(2)}, u32[]{:S(2)}) collective-permute-start(f32[16,11,11]{2,1,0:T(8,128)S(1)} %get-tuple-element.118), channel_id=1, source_target_pairs={{1,2},{3,4},{5,6},{9,10},{11,12},{13,14},{17,18},{19,20},{21,22},{... | collective-permute-start | bytes 23240 | tf_op jit(solution)/shard_map/ppermute | solution.py:71
  7.4 31.3 %collective-permute-start.1 = (f32[16,11,512]{2,1,0:T(8,128)}, f32[16,11,512]{2,1,0:T(8,128)S(1)}, u32[]{:S(2)}, u32[]{:S(2)}) collective-permute-start(f32[16,11,512]{2,1,0:T(8,128)} %get-tuple-element.120), channel_id=1, source_target_pairs={{0,2},{2,4},{4,6},{1,3},{3,5},{5,7},{8,10},{10,12},{12,14},{9,11},... | collective-permute-start | bytes 1081352 | tf_op jit(solution)/shard_map/ppermute | solution.py:69
  9.4 15.0 %collective-permute-start = (f32[16,11,11]{2,1,0:T(8,128)S(1)}, f32[16,11,11]{2,1,0:T(8,128)S(1)}, u32[]{:S(2)}, u32[]{:S(2)}) collective-permute-start(f32[16,11,11]{2,1,0:T(8,128)S(1)} %get-tuple-element.116), channel_id=1, source_target_pairs={{0,3},{2,5},{4,7},{8,11},{10,13},{12,15},{16,19},{18,21},{20,23},{... | collective-permute-start | bytes 23240 | tf_op jit(solution)/shard_map/ppermute | solution.py:71
  10.7 15.6 %collective-permute-start.7 = (f32[16,11,11]{2,1,0:T(8,128)}, f32[16,11,11]{2,1,0:T(8,128)}, u32[]{:S(2)}, u32[]{:S(2)}) collective-permute-start(f32[16,11,11]{2,1,0:T(8,128)} %get-tuple-element.119), channel_id=1, source_target_pairs={{3,0},{5,2},{7,4},{11,8},{13,10},{15,12},{19,16},{21,18},{23,20},{... | collective-permute-start | bytes 23240 | tf_op jit(solution)/shard_map/ppermute | solution.py:71
  15.6 23.0 %collective-permute-start.6 = (f32[16,11,512]{2,1,0:T(8,128)S(1)}, f32[16,11,512]{2,1,0:T(8,128)S(1)}, u32[]{:S(2)}, u32[]{:S(2)}) collective-permute-start(f32[16,11,512]{2,1,0:T(8,128)S(1)} %get-tuple-element.121), channel_id=1, source_target_pairs={{2,0},{4,2},{6,4},{3,1},{5,3},{7,5},{10,8},{12,10},{14,12},{11,9},... | collective-permute-start | bytes 1081352 | tf_op jit(solution)/shard_map/ppermute | solution.py:69
  23.1 15.5 %collective-permute-start.4 = (f32[16,32,11]{2,1,0:T(8,128)}, f32[16,32,11]{2,1,0:T(8,128)S(1)}, u32[]{:S(2)}, u32[]{:S(2)}) collective-permute-start(f32[16,32,11]{2,1,0:T(8,128)} %get-tuple-element.123), channel_id=1, source_target_pairs={{1,0},{3,2},{5,4},{7,6},{9,8},{11,10},{13,12},{15,14},{17,16},{19,... | collective-permute-start | bytes 67592 | tf_op jit(solution)/shard_map/ppermute | solution.py:66
  25.0 13.6 %collective-permute-start.3 = (f32[16,32,11]{2,1,0:T(8,128)S(1)}, f32[16,32,11]{2,1,0:T(8,128)S(1)}, u32[]{:S(2)}, u32[]{:S(2)}) collective-permute-start(f32[16,32,11]{2,1,0:T(8,128)S(1)} %get-tuple-element.122), channel_id=1, source_target_pairs={{0,1},{2,3},{4,5},{6,7},{8,9},{10,11},{12,13},{14,15},{16,17},{18,... | collective-permute-start | bytes 67592 | tf_op jit(solution)/shard_map/ppermute | solution.py:66
  26.3 12.3 %collective-permute-start.5 = (f32[16,11,11]{2,1,0:T(8,128)}, f32[16,11,11]{2,1,0:T(8,128)}, u32[]{:S(2)}, u32[]{:S(2)}) collective-permute-start(f32[16,11,11]{2,1,0:T(8,128)} %get-tuple-element.117), channel_id=1, source_target_pairs={{2,1},{4,3},{6,5},{10,9},{12,11},{14,13},{18,17},{20,19},{22,21},{... | collective-permute-start | bytes 23240 | tf_op jit(solution)/shard_map/ppermute | solution.py:71
  28.2 13.7 %copy-start.32 = (f32[16]{0:T(128)S(1)}, f32[16]{0:T(128)}, u32[]{:S(2)}) copy-start(f32[16]{0:T(128)} %get-tuple-element.76) | copy-start | bytes 196
  56.1 10.1 %collective-permute-start.10 = (f32[16,8,512]{2,1,0:T(8,128)S(1)}, f32[16,8,512]{2,1,0:T(8,128)S(1)}, u32[]{:S(2)}, u32[]{:S(2)}) collective-permute-start(f32[16,8,512]{2,1,0:T(8,128)S(1)} %get-tuple-element.113), channel_id=1, source_target_pairs={{0,24},{8,16},{16,8},{24,0},{1,25},{9,17},{17,9},{25,1},{2,26},{10... | collective-permute-start | bytes 786440 | tf_op jit(solution)/shard_map/ppermute | solution.py:33
  59.5 21.2 %collective-permute-start.9 = (f32[16,8,512]{2,1,0:T(8,128)S(1)}, f32[16,8,512]{2,1,0:T(8,128)S(1)}, u32[]{:S(2)}, u32[]{:S(2)}) collective-permute-start(f32[16,8,512]{2,1,0:T(8,128)S(1)} %get-tuple-element.114), channel_id=1, source_target_pairs={{0,16},{8,24},{16,0},{24,8},{1,17},{9,25},{17,1},{25,9},{2,18},{10... | collective-permute-start | bytes 786440 | tf_op jit(solution)/shard_map/ppermute | solution.py:33
  59.5 21.2 %collective-permute-start.8 = (f32[16,8,512]{2,1,0:T(8,128)S(1)}, f32[16,8,512]{2,1,0:T(8,128)S(1)}, u32[]{:S(2)}, u32[]{:S(2)}) collective-permute-start(f32[16,8,512]{2,1,0:T(8,128)S(1)} %get-tuple-element.115), channel_id=1, source_target_pairs={{0,8},{8,0},{16,24},{24,16},{1,9},{9,1},{17,25},{25,17},{2,10},{10... | collective-permute-start | bytes 786440 | tf_op jit(solution)/shard_map/ppermute | solution.py:33
  66.1 14.5 %copy-start.2 = (f32[16,8,512]{2,1,0:T(8,128)}, f32[16,8,512]{2,1,0:T(8,128)S(1)}, u32[]{:S(2)}) copy-start(f32[16,8,512]{2,1,0:T(8,128)S(1)} %collective-permute-done.10) | copy-start | bytes 786436
  87.8 8.5 %all-to-all-start = ((f32[4,8,512]{2,1,0:T(8,128)}), f32[4,8,512]{2,1,0:T(8,128)S(1)}, u32[]{:S(2)}, u32[]{:S(2)}) async-start(f32[4,8,512]{2,1,0:T(8,128)} %tile.2), calls=%async_computation | async-start | bytes 131072 | tf_op jit(solution)/shard_map/all_to_all | solution.py:156
  96.3 12.3 %collective-permute-start.15 = (f32[32,4]{1,0:T(8,128)S(1)}, f32[32,4]{1,0:T(8,128)S(1)}, u32[]{:S(2)}, u32[]{:S(2)}) collective-permute-start(f32[32,4]{1,0:T(8,128)S(1)} %get-tuple-element.149), channel_id=1, source_target_pairs={{1,0},{3,2},{5,4},{7,6},{9,8},{11,10},{13,12},{15,14},{17,16},{19,... | collective-permute-start | bytes 1544 | tf_op jit(solution)/shard_map/ppermute | solution.py:66
  97.7 15.3 %collective-permute-start.14 = (f32[32,4]{1,0:T(8,128)S(1)}, f32[32,4]{1,0:T(8,128)S(1)}, u32[]{:S(2)}, u32[]{:S(2)}) collective-permute-start(f32[32,4]{1,0:T(8,128)S(1)} %get-tuple-element.148), channel_id=1, source_target_pairs={{0,1},{2,3},{4,5},{6,7},{8,9},{10,11},{12,13},{14,15},{16,17},{18,... | collective-permute-start | bytes 1544 | tf_op jit(solution)/shard_map/ppermute | solution.py:66
  99.0 16.0 %collective-permute-start.13 = (f32[4,4]{1,0:T(4,128)S(1)}, f32[4,4]{1,0:T(4,128)S(1)}, u32[]{:S(2)}, u32[]{:S(2)}) collective-permute-start(f32[4,4]{1,0:T(4,128)S(1)} %get-tuple-element.145), channel_id=1, source_target_pairs={{1,2},{3,4},{5,6},{9,10},{11,12},{13,14},{17,18},{19,20},{21,22},{... | collective-permute-start | bytes 200 | tf_op jit(solution)/shard_map/ppermute | solution.py:71
  105.4 15.4 %collective-permute-start.12 = (f32[4,512]{1,0:T(4,128)S(1)}, f32[4,512]{1,0:T(4,128)S(1)}, u32[]{:S(2)}, u32[]{:S(2)}) collective-permute-start(f32[4,512]{1,0:T(4,128)S(1)} %get-tuple-element.146), channel_id=1, source_target_pairs={{0,2},{2,4},{4,6},{1,3},{3,5},{5,7},{8,10},{10,12},{12,14},{9,11},... | collective-permute-start | bytes 24584 | tf_op jit(solution)/shard_map/ppermute | solution.py:69
  107.4 9.1 %collective-permute-start.11 = (f32[4,4]{1,0:T(4,128)S(1)}, f32[4,4]{1,0:T(4,128)S(1)}, u32[]{:S(2)}, u32[]{:S(2)}) collective-permute-start(f32[4,4]{1,0:T(4,128)S(1)} %get-tuple-element.142), channel_id=1, source_target_pairs={{0,3},{2,5},{4,7},{8,11},{10,13},{12,15},{16,19},{18,21},{20,23},{... | collective-permute-start | bytes 200 | tf_op jit(solution)/shard_map/ppermute | solution.py:71
  108.7 7.8 %collective-permute-start.18 = (f32[4,4]{1,0:T(4,128)S(1)}, f32[4,4]{1,0:T(4,128)S(1)}, u32[]{:S(2)}, u32[]{:S(2)}) collective-permute-start(f32[4,4]{1,0:T(4,128)S(1)} %get-tuple-element.143), channel_id=1, source_target_pairs={{3,0},{5,2},{7,4},{11,8},{13,10},{15,12},{19,16},{21,18},{23,20},{... | collective-permute-start | bytes 200 | tf_op jit(solution)/shard_map/ppermute | solution.py:71
  112.9 7.8 %collective-permute-start.17 = (f32[4,512]{1,0:T(4,128)S(1)}, f32[4,512]{1,0:T(4,128)S(1)}, u32[]{:S(2)}, u32[]{:S(2)}) collective-permute-start(f32[4,512]{1,0:T(4,128)S(1)} %get-tuple-element.147), channel_id=1, source_target_pairs={{2,0},{4,2},{6,4},{3,1},{5,3},{7,5},{10,8},{12,10},{14,12},{11,9},... | collective-permute-start | bytes 24584 | tf_op jit(solution)/shard_map/ppermute | solution.py:69
  115.0 5.8 %collective-permute-start.16 = (f32[4,4]{1,0:T(4,128)S(1)}, f32[4,4]{1,0:T(4,128)S(1)}, u32[]{:S(2)}, u32[]{:S(2)}) collective-permute-start(f32[4,4]{1,0:T(4,128)S(1)} %get-tuple-element.144), channel_id=1, source_target_pairs={{2,1},{4,3},{6,5},{10,9},{12,11},{14,13},{18,17},{20,19},{22,21},{... | collective-permute-start | bytes 200 | tf_op jit(solution)/shard_map/ppermute | solution.py:71
  (45 other events, 384.5 us)
